TPU v7x, 512 devices: a whole 4x8x8 slice. The times are simulated.
512 devices in a mesh: seq: 64 (over z, x, core), head: 8 (over y).
Axes of the slice: x: 4, y: 8, z: 8, core: 2. Of those that a mesh axis runs over, the one named last changes fastest.
Arguments:
- projected: float32 [65536, 2560], P(('seq', 'head')), may hold values from -6 to 6
- out_grads: float32 [65536, 2048], P(('seq', 'head')), may hold values from -6 to 6
- conv_weight: float32 [3, 2560], replicated, may hold values from -2.4 to 2.4
- doc_lengths: int32 [16], replicated, may hold values from 1 to 32768, 65536 in all
Outputs:
- grad_projected: float32 [65536, 2560], P(('seq', 'head'))
- grad_conv: float32 [3, 2560], replicated
Inputs may be any that keep to these rules, and one draw needn't show every extreme that they name: `doc_lengths`: the 16 documents fill the 65536 tokens end to end; the longest holds exactly half of 65536 tokens.
All inputs are finite; a program needn't handle non-finite values.
Results may differ from a plain program's by a relative error of at most 0.0003.
Values sent between devices are 32-bit elements; how exact they have to be, the bound alone decides.
No kernel may reach another device: no remote copies, remote signals or barrier semaphores. Data moves between devices by JAX's collectives and lax.ppermute only.
A program may use at most 128 MiB of HBM per device.

v0:
```python
import math
import jax
import jax.numpy as jnp
import numpy as np
from jax import lax
from jax.sharding import PartitionSpec as P

KEY_DIM = 16
HEAD_DIM = 128
HIGHEST = lax.Precision.HIGHEST


def segment_sum(gathered, flags, here, reverse):
    count = gathered.shape[0]
    index = jnp.arange(count, dtype=jnp.int32)
    started = flags > 0.5
    if reverse:
        bound = jnp.min(jnp.where((index > here) & started, index, count - 1))
        take = (index > here) & (index <= bound)
    else:
        bound = jnp.max(jnp.where((index < here) & started, index, 0))
        take = (index >= bound) & (index < here)
    return jnp.sum(jnp.where(take[:, None], gathered, 0.0), axis=0)


def carried_in(state, norm, extra, flags, axis, reverse):
    here = lax.axis_index(axis)
    size = state.size
    packed = jnp.concatenate([state.reshape(-1), norm.reshape(-1), extra])
    width = 128
    padded = jnp.pad(packed, (0, -packed.shape[0] % width)).reshape(-1, width)
    gathered = lax.all_gather(padded, axis).reshape(lax.axis_size(axis), -1)
    if flags is None:
        flags = gathered[:, packed.shape[0] - 1]
    total = segment_sum(gathered[:, : size + norm.size], flags, here, reverse)
    return (total[:size].reshape(state.shape), total[size:].reshape(norm.shape), flags)


def passed_along(value, axis, steps):
    count = lax.axis_size(axis)
    initial, last = (max(0, -steps), min(count, count - steps))
    return lax.ppermute(value, axis, [(source, source + steps) for source in range(initial, last)])


def feature_map(columns):
    key_size = columns.shape[1]
    upper_i, upper_j = np.triu_indices(key_size)
    factors = np.where(upper_i == upper_j, 1.0 / math.sqrt(2.0), 1.0).astype(np.float32)
    products = columns[:, upper_i, :] * columns[:, upper_j, :] * jnp.asarray(factors)[None, :, None]
    constant = jnp.ones((columns.shape[0], 1, columns.shape[2]), jnp.float32)
    return jnp.concatenate([constant, columns, products], axis=1)


def doc_place(doc_lengths, anchor, amount):
    positions = anchor + jnp.arange(amount, dtype=jnp.int32)
    starts = jnp.cumsum(doc_lengths) - doc_lengths
    begins = jnp.max(jnp.where(starts[None, :] <= positions[:, None], starts[None, :], 0), axis=1)
    return (begins, positions - begins)


def conv_forward(signal, leading, weights, offsets):
    row_count = signal.shape[0]
    behind = jnp.concatenate([leading, signal], axis=0)
    back_one = behind[1 : row_count + 1] * (offsets[0:row_count] >= 1).astype(jnp.float32)[:, None]
    back_two = behind[0:row_count] * (offsets[0:row_count] >= 2).astype(jnp.float32)[:, None]
    return weights[0] * signal + weights[1] * back_one + weights[2] * back_two


def conv_backward(grad_rows, trailing, signal, leading, weights, offsets):
    row_count = grad_rows.shape[0]
    ahead_rows = jnp.concatenate([grad_rows, trailing], axis=0)
    ahead_one = (
        ahead_rows[1 : row_count + 1]
        * (offsets[1 : row_count + 1] >= 1).astype(jnp.float32)[:, None]
    )
    ahead_two = (
        ahead_rows[2 : row_count + 2]
        * (offsets[2 : row_count + 2] >= 2).astype(jnp.float32)[:, None]
    )
    grad_signal = weights[0] * grad_rows + weights[1] * ahead_one + weights[2] * ahead_two
    behind = jnp.concatenate([leading, signal], axis=0)
    own_one = (offsets[0:row_count] >= 1).astype(jnp.float32)[:, None]
    own_two = (offsets[0:row_count] >= 2).astype(jnp.float32)[:, None]
    grad_weights = jnp.stack(
        [
            jnp.sum(grad_rows * signal, axis=0),
            jnp.sum(grad_rows * behind[1 : row_count + 1] * own_one, axis=0),
            jnp.sum(grad_rows * behind[0:row_count] * own_two, axis=0),
        ],
        axis=0,
    )
    return (grad_signal, grad_weights)


def attention_grads(mixed_rows, out_flat, begins, stretch_start):
    length = mixed_rows.shape[0]
    head_width = 2 * KEY_DIM + HEAD_DIM
    local_heads = mixed_rows.shape[1] // head_width
    block_len = min(128, length)
    blocks = length // block_len
    scale_key = KEY_DIM ** (-0.25)
    shaped = mixed_rows.reshape(length, local_heads, head_width)
    query_cols = jnp.transpose(shaped[:, :, :KEY_DIM], (1, 2, 0)) * scale_key
    key_cols = jnp.transpose(shaped[:, :, KEY_DIM : 2 * KEY_DIM], (1, 2, 0)) * scale_key
    values = shaped[:, :, 2 * KEY_DIM :]
    upstream = out_flat.reshape(length, local_heads, HEAD_DIM)
    query_feat, query_pull = jax.vjp(feature_map, query_cols)
    key_feat, key_pull = jax.vjp(feature_map, key_cols)
    feat_count = query_feat.shape[1]
    last_begin = begins[length - 1]
    has_start = (last_begin >= stretch_start).astype(jnp.float32).reshape(1)
    tail_mask = (begins == last_begin).astype(jnp.float32)
    tail_feat = key_feat * tail_mask[None, None, :]
    tail_state = jnp.einsum("hfl,lhe->hfe", tail_feat, values, precision=HIGHEST)
    tail_norm = jnp.sum(tail_feat, axis=2)
    prefix = carried_in(tail_state, tail_norm, has_start, None, "seq", False)
    flags = prefix[2]
    causal = jnp.arange(block_len)[:, None] >= jnp.arange(block_len)[None, :]
    indices = jnp.arange(blocks, dtype=jnp.int32)

    def forward_block(carried, block_index):
        carry_state, carry_norm = carried
        offset_rows = block_index * block_len
        block_start = stretch_start + offset_rows
        query_blk = lax.dynamic_slice_in_dim(query_feat, offset_rows, block_len, 2)
        key_blk = lax.dynamic_slice_in_dim(key_feat, offset_rows, block_len, 2)
        value_blk = lax.dynamic_slice_in_dim(values, offset_rows, block_len, 0)
        doc_blk = lax.dynamic_slice_in_dim(begins, offset_rows, block_len, 0)
        allowed = causal & (doc_blk[:, None] == doc_blk[None, :])
        scores = jnp.where(
            allowed[None], jnp.einsum("hft,hfs->hts", query_blk, key_blk, precision=HIGHEST), 0.0
        )
        from_carry = (doc_blk < block_start).astype(jnp.float32)
        numerator = jnp.einsum("hts,she->the", scores, value_blk, precision=HIGHEST) + from_carry[
            :, None, None
        ] * jnp.einsum("hft,hfe->the", query_blk, carry_state, precision=HIGHEST)
        denominator = jnp.sum(scores, axis=2) + from_carry[None, :] * jnp.einsum(
            "hft,hf->ht", query_blk, carry_norm, precision=HIGHEST
        )
        block_tail = (doc_blk == doc_blk[block_len - 1]).astype(jnp.float32)
        carry_keep = (doc_blk[block_len - 1] < block_start).astype(jnp.float32)
        tail_keys = key_blk * block_tail[None, None, :]
        next_state = (
            jnp.einsum("hfs,she->hfe", tail_keys, value_blk, precision=HIGHEST)
            + carry_keep * carry_state
        )
        next_norm = jnp.sum(tail_keys, axis=2) + carry_keep * carry_norm
        return ((next_state, next_norm), (numerator, denominator, carry_state, carry_norm, scores))

    forward_out = lax.scan(forward_block, (prefix[0], prefix[1]), indices)
    numerators, denominators, states, norms, kept_scores = forward_out[1]
    denom_rows = jnp.transpose(denominators, (0, 2, 1)).reshape(length, local_heads)
    attended = numerators.reshape(length, local_heads, HEAD_DIM) / denom_rows[:, :, None]
    grad_num = upstream / denom_rows[:, :, None]
    scalar_grad = -jnp.sum(upstream * attended, axis=2) / denom_rows
    lead_mask = (begins < stretch_start).astype(jnp.float32)
    lead_feat = query_feat * lead_mask[None, None, :]
    lead_state = jnp.einsum("hfl,lhe->hfe", lead_feat, grad_num, precision=HIGHEST)
    lead_norm = jnp.einsum("hfl,lh->hf", lead_feat, scalar_grad, precision=HIGHEST)
    suffix = carried_in(lead_state, lead_norm, jnp.zeros((0,), jnp.float32), flags, "seq", True)

    def backward_block(carried, inputs):
        back_state, back_norm = carried
        block_index, carry_state, carry_norm, scores = inputs
        offset_rows = block_index * block_len
        block_start = stretch_start + offset_rows
        query_blk = lax.dynamic_slice_in_dim(query_feat, offset_rows, block_len, 2)
        key_blk = lax.dynamic_slice_in_dim(key_feat, offset_rows, block_len, 2)
        value_blk = lax.dynamic_slice_in_dim(values, offset_rows, block_len, 0)
        doc_blk = lax.dynamic_slice_in_dim(begins, offset_rows, block_len, 0)
        grad_blk = lax.dynamic_slice_in_dim(grad_num, offset_rows, block_len, 0)
        scalar_blk = lax.dynamic_slice_in_dim(scalar_grad, offset_rows, block_len, 0)
        scalar_cols = scalar_blk.T
        allowed = causal & (doc_blk[:, None] == doc_blk[None, :])
        dscores = jnp.where(
            allowed[None],
            jnp.einsum("the,she->hts", grad_blk, value_blk, precision=HIGHEST)
            + scalar_cols[:, :, None],
            0.0,
        )
        from_carry = (doc_blk < block_start).astype(jnp.float32)
        block_tail = (doc_blk == doc_blk[block_len - 1]).astype(jnp.float32)
        carry_keep = (doc_blk[block_len - 1] < block_start).astype(jnp.float32)
        grad_query = jnp.einsum("hts,hfs->hft", dscores, key_blk, precision=HIGHEST) + from_carry[
            None, None, :
        ] * (
            jnp.einsum("hfe,the->hft", carry_state, grad_blk, precision=HIGHEST)
            + carry_norm[:, :, None] * scalar_cols[:, None, :]
        )
        grad_key = jnp.einsum("hts,hft->hfs", dscores, query_blk, precision=HIGHEST) + block_tail[
            None, None, :
        ] * (
            jnp.einsum("hfe,she->hfs", back_state, value_blk, precision=HIGHEST)
            + back_norm[:, :, None]
        )
        grad_value = jnp.einsum("hts,the->she", scores, grad_blk, precision=HIGHEST) + block_tail[
            :, None, None
        ] * jnp.einsum("hfs,hfe->she", key_blk, back_state, precision=HIGHEST)
        lead_blk = query_blk * from_carry[None, None, :]
        next_state = (
            jnp.einsum("hft,the->hfe", lead_blk, grad_blk, precision=HIGHEST)
            + carry_keep * back_state
        )
        next_norm = (
            jnp.einsum("hft,th->hf", lead_blk, scalar_blk, precision=HIGHEST)
            + carry_keep * back_norm
        )
        return ((next_state, next_norm), (grad_query, grad_key, grad_value))

    swept_back = lax.scan(
        backward_block, (suffix[0], suffix[1]), (indices, states, norms, kept_scores), reverse=True
    )
    grad_qblocks, grad_kblocks, grad_vblocks = swept_back[1]
    query_grad = jnp.transpose(grad_qblocks, (1, 2, 0, 3)).reshape(local_heads, feat_count, length)
    key_grad = jnp.transpose(grad_kblocks, (1, 2, 0, 3)).reshape(local_heads, feat_count, length)
    value_grad = grad_vblocks.reshape(length, local_heads, HEAD_DIM)
    query_in = jnp.transpose(query_pull(query_grad)[0] * scale_key, (2, 0, 1))
    key_in = jnp.transpose(key_pull(key_grad)[0] * scale_key, (2, 0, 1))
    return jnp.concatenate([query_in, key_in, value_grad], axis=2).reshape(
        length, local_heads * head_width
    )


def on_device(projected, out_grads, conv_weight, doc_lengths):
    row_count = projected.shape[0]
    head_count = lax.axis_size("head")
    seq_index = lax.axis_index("seq")
    head_index = lax.axis_index("head")
    group_len = row_count * head_count
    token_base = (seq_index * head_count + head_index) * row_count
    stretch_start = seq_index * group_len
    token_begins, token_offsets = doc_place(doc_lengths, token_base, row_count + 2)
    leading = passed_along(projected[row_count - 2 :], ("seq", "head"), 1)
    outgoing = conv_forward(projected, leading, conv_weight, token_offsets)
    arrived, upstream = (
        lax.all_to_all(outgoing, "head", split_axis=1, concat_axis=0, tiled=True),
        lax.all_to_all(out_grads, "head", split_axis=1, concat_axis=0, tiled=True),
    )
    group_begins, group_offsets = doc_place(doc_lengths, stretch_start, group_len + 2)
    grad_mixed = attention_grads(arrived, upstream, group_begins[:group_len], stretch_start)
    returned = lax.all_to_all(grad_mixed, "head", split_axis=0, concat_axis=1, tiled=True)
    trailing = passed_along(returned[:2], ("seq", "head"), -1)
    grad_projected, weight_part = conv_backward(
        returned, trailing, projected, leading, conv_weight, token_offsets
    )
    grad_conv = lax.psum(weight_part, ("seq", "head"))
    return (grad_projected, grad_conv)


def solution(mesh):
    return jax.shard_map(
        on_device,
        mesh=mesh,
        in_specs=(P(("seq", "head"), None), P(("seq", "head"), None), P(), P()),
        out_specs=(P(("seq", "head"), None), P()),
        check_vma=False,
    )
```

profile of v0, /device:TPU:1, one launch (start us, length us, event | category | flops | bytes accessed | tf_op | source)
XLA Modules:
  0.0 737.0 jit_solution(17403635177316418319)
XLA Ops:
  8.1 4.0 collective-permute-start
  17.0 3.1 multiply_add_fusion.1
  20.1 6.1 all-to-all-start
  28.1 32.9 %all-to-all-done = f32[128,8,320]{0,2,1:T(8,128)S(1)} async-done(((f32[128,8,320]{0,2,1:T(8,128)}), f32[128,8,320]{0,2,1:T(8,128)S(1)}, u32[]{:S(2)}, u32[]{:S(2)}) %all-to-all-start) | async-done | bytes 1310752 | tf_op jit(solution)/shard_map/all_to_all | solution.py:236
  65.0 3.0 gather_fusion
  68.1 3.1 gather_fusion.1
  71.1 3.0 gather_fusion.2
  74.2 3.0 gather_fusion.3
  77.2 3.4 fusion.89
  80.6 4.3 fusion.98
  88.8 3.6 all-to-all-start.1
  92.7 28.9 %all-to-all-done.1 = f32[128,8,256]{0,2,1:T(8,128)S(1)} async-done(((f32[128,8,256]{0,2,1:T(8,128)}), f32[128,8,256]{0,2,1:T(8,128)S(1)}, u32[]{:S(2)}, u32[]{:S(2)}) %all-to-all-start.1) | async-done | bytes 1048608 | tf_op jit(solution)/shard_map/all_to_all | solution.py:237
  123.2 2.4 reshape.233
  128.4 2.5 copy.272
  131.0 48.2 %all-gather.3.cloned.1.call-done = f32[64,309,128]{2,1,0:T(8,128)} async-done(((f32[1,309,128]{2,1,0:T(8,128)}), f32[64,309,128]{2,1,0:T(8,128)}) %all-gather.3.cloned.1.call-update) | async-done | bytes 10125328 | tf_op jit(solution)/shard_map/all_gather | solution.py:32
  179.2 5.7 copy.305
  188.8 110.3 %while.46 = (s32[]{:T(128)}, f32[2,153,128]{2,1,0:T(8,128)S(1)}, f32[2,153]{1,0:T(2,128)S(1)}, f32[8,128,2,128]{1,0,3,2:T(8,128)}, f32[8,2,128]{2,1,0:T(2,128)S(...) while((s32[]{:T(128)}, f32[2,153,128]{2,1,0:T(8,128)S(1)}, ...), condition=%wide.region_10.11_spmd.clone, body=%wide.region_7.10_spmd.clone.sunk | while | flops 231664960 | bytes 3280461 | solution.py:150
  192.8 4.8 dynamic_update_slice.74
  206.6 4.8 dynamic_update_slice.74
  220.4 4.8 dynamic_update_slice.74
  234.2 4.8 dynamic_update_slice.74
  248.0 4.8 dynamic_update_slice.74
  261.8 4.8 dynamic_update_slice.74
  275.6 4.8 dynamic_update_slice.74
  289.3 4.8 dynamic_update_slice.74
  299.0 2.4 reshape.237
  306.0 2.8 fusion.81
  310.3 88.0 %all-gather.5.cloned.1.call-done = f32[64,309,128]{2,1,0:T(8,128)} async-done(((f32[1,309,128]{2,1,0:T(8,128)}), f32[64,309,128]{2,1,0:T(8,128)}) %all-gather.5.cloned.1.call-update) | async-done | bytes 10125328 | tf_op jit(solution)/shard_map/all_gather | solution.py:32
  398.3 5.7 copy.304
  408.5 112.2 %while.47 = (s32[]{:T(128)}, f32[2,153,128]{2,1,0:T(8,128)S(1)}, f32[2,153]{1,0:T(2,128)S(1)}, f32[8,2,153,128]{3,2,1,0:T(8,128)}, f32[8,2,153,128]{3,2,1,0:T(8,...) while((s32[]{:T(128)}, f32[2,153,128]{2,1,0:T(8,128)S(1)}, ...), condition=%wide.region_14.15_spmd.clone, body=%wide.region_13.14_spmd.clone.sunk | while | flops 462717824 | bytes 4866477 | solution.py:210
  415.4 2.0 fusion.190
  443.4 2.0 fusion.190
  457.4 2.0 fusion.190
  485.4 2.0 fusion.190
  499.4 2.0 fusion.190
  513.4 2.0 fusion.190
  520.8 2.0 copy.242
  526.3 2.0 reshape.243
  529.4 6.0 fusion.85
  535.3 14.0 %scatter_fusion = f32[2,16,1024]{2,0,1:T(2,128)S(1)} fusion(f32[2,16,1024]{2,0,1:T(2,128)S(1)} %split.16, s32[136]{0:T(256)S(1)} %copy-done.16, f32[136,2,1024]{2,1,0:T(2,128)} %get-tuple-element.822), kind=kCustom, calls=%fused_computation.4 | custom fusion | flops 278528 | bytes 3342880 | tf_op jit(solution)/shard_map/transpose(jvp())/scatter-add | solution.py:49
  549.4 7.6 %scatter_fusion.1 = f32[2,16,1024]{2,0,1:T(2,128)S(1)} fusion(f32[2,16,1024]{2,0,1:T(2,128)S(1)} %broadcast.144.clone.1, s32[136]{0:T(256)S(1)} %copy-done.17, f32[136,2,1024]{2,1,0:T(2,128)S(1)} %copy-done.13), kind=kCustom, calls=%fused_computation.5 | custom fusion | flops 278528 | bytes 3342880 | tf_op jit(solution)/shard_map/transpose(jvp())/scatter-add | solution.py:49
  558.4 7.6 %scatter_fusion.3 = f32[2,16,1024]{2,0,1:T(2,128)S(1)} fusion(f32[2,16,1024]{2,0,1:T(2,128)S(1)} %broadcast.144.clone, s32[136]{0:T(256)S(1)} %copy-done.17, f32[136,2,1024]{2,1,0:T(2,128)S(1)} %copy-done.12), kind=kCustom, calls=%fused_computation.7 | custom fusion | flops 278528 | bytes 3342880 | tf_op jit(solution)/shard_map/transpose(jvp())/scatter-add | solution.py:49
  566.0 7.3 scatter_fusion.2
  574.8 3.0 pad_maximum_fusion
  581.3 41.0 %all_to_all.51 = f32[8,128,320]{1,2,0:T(8,128)S(1)} all-to-all(f32[8,128,320]{1,2,0:T(8,128)S(1)} %copy.248), channel_id=1, replica_groups=mesh['seq'=64,'head'=8] {'head'}, dimensions={0} | all-to-all | bytes 2621440 | tf_op jit(solution)/shard_map/all_to_all | solution.py:241
  622.3 2.1 multiply_reduce_fusion.2
  626.8 95.7 %psum.7 = f32[3,2560]{1,0:T(4,128)} all-reduce(f32[3,2560]{1,0:T(4,128)S(1)} %pad_maximum_fusion.5), channel_id=1, replica_groups=mesh['seq'=64,'head'=8] {'seq','head'}, use_global_device_ids=true, to_apply=%region_22.23 | all-reduce | flops 7680 | bytes 61440 | tf_op jit(solution)/shard_map/psum | solution.py:246
  724.1 4.3 fusion.75
  (413 shorter events, 200.4 us)
Async XLA Ops:
  8.1 8.5 %collective-permute-start = (f32[2,2560]{1,0:T(2,128)S(1)}, f32[2,2560]{1,0:T(2,128)S(1)}, u32[]{:S(2)}, u32[]{:S(2)}) collective-permute-start(f32[2,2560]{1,0:T(2,128)S(1)} %slice.116), channel_id=1, source_target_pairs={{0,1},{1,2},{2,3},{3,4},{4,5},{5,6},{6,7},{7,8},{8,9},{9,10},{10,1... | collective-permute-start | bytes 61448 | tf_op jit(solution)/shard_map/ppermute | solution.py:42
  16.6 3.5 copy-start.3
  17.0 3.1 copy-start.5
  20.1 7.4 %copy-start.17 = (s32[136]{0:T(256)S(1)}, s32[136]{0:T(256)}, u32[]{:S(2)}) copy-start(s32[136]{0:T(256)} %constant.158) | copy-start | bytes 1636
  20.1 7.4 %copy-start.16 = (s32[136]{0:T(256)S(1)}, s32[136]{0:T(256)}, u32[]{:S(2)}) copy-start(s32[136]{0:T(256)} %constant.159) | copy-start | bytes 1636
  20.1 40.9 %all-to-all-start = ((f32[128,8,320]{0,2,1:T(8,128)}), f32[128,8,320]{0,2,1:T(8,128)S(1)}, u32[]{:S(2)}, u32[]{:S(2)}) async-start(f32[128,8,320]{0,2,1:T(8,128)} %bitcast.248), calls=%async_computation | async-start | bytes 2621440 | tf_op jit(solution)/shard_map/all_to_all | solution.py:236
  26.2 153.0 %all-gather.3.cloned.1.call-start = ((), (), s32[]{:S(2)}) async-start(), calls=%async_computation.3 | async-start | bytes 10383360 | tf_op jit(solution)/shard_map/all_gather | solution.py:32
  26.3 66.3 %copy-start.15 = (s32[1026]{0:T(1024)}, s32[1026]{0:T(1024)S(1)}, u32[]{:S(2)}) copy-start(s32[1026]{0:T(1024)S(1)} %select_reduce_fusion) | copy-start | bytes 12316
  74.2 3.0 copy-start.18
  84.9 2.6 copy-start.14
  88.8 32.7 %all-to-all-start.1 = ((f32[128,8,256]{0,2,1:T(8,128)}), f32[128,8,256]{0,2,1:T(8,128)S(1)}, u32[]{:S(2)}, u32[]{:S(2)}) async-start(f32[128,8,256]{0,2,1:T(8,128)} %bitcast.256), calls=%async_computation.1 | async-start | bytes 2097152 | tf_op jit(solution)/shard_map/all_to_all | solution.py:237
  92.4 305.8 %all-gather.5.cloned.1.call-start = ((), (), s32[]{:S(2)}) async-start(), calls=%async_computation.4 | async-start | bytes 10383360 | tf_op jit(solution)/shard_map/all_gather | solution.py:32
  125.5 1.7 copy-start.10
  126.6 1.4 copy-start.9
  187.4 1.3 slice-start.1
  301.4 2.9 copy-start.2
  303.3 1.0 copy-start
  522.8 1.7 copy-start.8
  526.3 3.1 copy-start.7
  528.3 7.1 copy-start.1
  535.3 14.0 %copy-start.13 = (f32[136,2,1024]{2,1,0:T(2,128)S(1)}, f32[136,2,1024]{2,1,0:T(2,128)}, u32[]{:S(2)}) copy-start(f32[136,2,1024]{2,1,0:T(2,128)} %get-tuple-element.821) | copy-start | bytes 3342340
  557.0 1.4 copy-start.12
  558.4 7.6 %slice-start = ((f32[2,153,1024]{2,0,1:T(2,128)}), f32[2,16,1024]{2,0,1:T(2,128)S(1)}, s32[]{:S(2)}) async-start(f32[2,153,1024]{2,0,1:T(2,128)} %copy-done.1), calls=%async_computation.5 | async-start | bytes 262144 | tf_op jit(solution)/shard_map/transpose(jvp())/split | solution.py:51
  558.4 7.6 %copy-start.11 = (f32[136,2,1024]{2,1,0:T(2,128)S(1)}, f32[136,2,1024]{2,1,0:T(2,128)}, u32[]{:S(2)}) copy-start(f32[136,2,1024]{2,1,0:T(2,128)} %get-tuple-element.833) | copy-start | bytes 3342340
  581.3 41.0 %copy-start.4 = (f32[128,2560]{0,1:T(8,128)S(1)}, f32[128,2560]{0,1:T(8,128)}, u32[]{:S(2)}) copy-start(f32[128,2560]{0,1:T(8,128)} %copy-done.3) | copy-start | bytes 3932164
  581.3 41.0 %copy-start.6 = (f32[2,2560]{0,1:T(8,128)S(1)}, f32[2,2560]{0,1:T(8,128)}, u32[]{:S(2)}) copy-start(f32[2,2560]{0,1:T(8,128)} %copy-done.5) | copy-start | bytes 61444
  624.9 97.7 %collective-permute-start.1 = (f32[2,2560]{1,0:T(2,128)S(1)}, f32[2,2560]{1,0:T(2,128)S(1)}, u32[]{:S(2)}, u32[]{:S(2)}) collective-permute-start(f32[2,2560]{1,0:T(2,128)S(1)} %copy.249), channel_id=1, source_target_pairs={{1,0},{2,1},{3,2},{4,3},{5,4},{6,5},{7,6},{8,7},{9,8},{10,9},{11,1... | collective-permute-start | bytes 61448 | tf_op jit(solution)/shard_map/ppermute | solution.py:42
Sparse Core Ops, SparseCore 0:
  87.6 91.5 all-gather.2
  309.7 88.5 all-gather.4
where the time goes:
time: 743 us; the launch traced here: 737 us
  waiting for transfers between devices  198 us (27%)
  local copies, waits for them, and re-layouts  146 us (20%)
  blocking collectives  137 us (18%)
  matrix products  117 us (16%)
  other arithmetic  85.8 us (12%)
  loops' own time  22.4 us (3%)
  starting transfers between devices  15.8 us (2%)
  between operations  15.5 us (2%)
    all_gather x2, waiting for transfers between devices, carried_in(): gathered = lax.all_gather(padded, axis).reshape(lax.axis_size(axis), -1)  136 us
    psum x1, blocking collectives, on_device(): grad_conv = lax.psum(weight_part, ('seq', 'head'))  95.7 us
    dynamic_update_slice x48, local copies, waits for them, and re-layouts, attention_grads(): forward_out = lax.scan(forward_block, (prefix[0], prefix[1]), indices)  55 us
    all_to_all x1, blocking collectives, on_device(): lax.all_to_all(grad_mixed, 'head', split_axis=0, concat_axis=1, tiled=True)  41 us
    all_to_all x1, waiting for transfers between devices, on_device(): lax.all_to_all(outgoing, 'head', split_axis=1, concat_axis=0, tiled=True)  32.9 us
    all_to_all x1, waiting for transfers between devices, on_device(): lax.all_to_all(out_grads, 'head', split_axis=1, concat_axis=0, tiled=True)  28.9 us
    unnamed x48, local copies, waits for them, and re-layouts  23.9 us
    scatter-add x2, other arithmetic, feature_map(): columns[:, upper_j, :]  21.3 us
  transfers between devices with their start and end apart: 6, of which 4 were waited for; matrix products, arithmetic and copies ran while one was open for 2% of the time, Pallas kernels for 0%

commit v1 on v0

--- a/solution.py
+++ b/solution.py
@@ -243,7 +243,7 @@
     grad_projected, weight_part = conv_backward(
         returned, trailing, projected, leading, conv_weight, token_offsets
     )
-    grad_conv = lax.psum(weight_part, ("seq", "head"))
+    grad_conv = jnp.sum(lax.all_gather(weight_part, ("seq", "head")), axis=0)
     return (grad_projected, grad_conv)
 
 

time: 743 us -> 784 us (1.055)
  waiting for transfers between devices: 198 us -> 318 us
  blocking collectives: 137 us -> 40.8 us
  other arithmetic: 85.8 us -> 99.4 us
    all_gather x0 -> x1, waiting for transfers between devices: none -> 121 us  [on_device(): grad_conv = jnp.sum(lax.all_gather(weight_part, ('seq', 'head')), axis=0)]
    psum x1 -> x0, blocking collectives: 95.7 us -> none  [on_device(): grad_conv = lax.psum(weight_part, ('seq', 'head'))]
    reduce_sum x0 -> x1, other arithmetic: none -> 12.6 us  [on_device(): grad_conv = jnp.sum(lax.all_gather(weight_part, ('seq', 'head')), axis=0)]
    unnamed x48 -> x70, local copies, waits for them, and re-layouts: 23.9 us -> 24.5 us
  transfers between devices with their start and end apart: 6 -> 7, of which waited for: 4 -> 6; matrix products, arithmetic and copies ran while one was open for 2% -> 3% of each run, Pallas kernels for 0% -> 0%
where the time goes in v1:
time: 784 us; the launch traced here: 773 us
  waiting for transfers between devices  318 us (41%)
  local copies, waits for them, and re-layouts  143 us (18%)
  matrix products  117 us (15%)
  other arithmetic  99.4 us (13%)
  blocking collectives  40.8 us (5%)
  loops' own time  23.5 us (3%)
  starting transfers between devices  16.4 us (2%)
  between operations  15.6 us (2%)
    all_gather x2, waiting for transfers between devices, carried_in(): gathered = lax.all_gather(padded, axis).reshape(lax.axis_size(axis), -1)  133 us
    all_gather x1, waiting for transfers between devices, on_device(): grad_conv = jnp.sum(lax.all_gather(weight_part, ('seq', 'head')), axis=0)  121 us
    dynamic_update_slice x48, local copies, waits for them, and re-layouts, attention_grads(): forward_out = lax.scan(forward_block, (prefix[0], prefix[1]), indices)  55.1 us
    all_to_all x1, blocking collectives, on_device(): lax.all_to_all(grad_mixed, 'head', split_axis=0, concat_axis=1, tiled=True)  40.8 us
    all_to_all x1, waiting for transfers between devices, on_device(): lax.all_to_all(outgoing, 'head', split_axis=1, concat_axis=0, tiled=True)  32.8 us
    all_to_all x1, waiting for transfers between devices, on_device(): lax.all_to_all(out_grads, 'head', split_axis=1, concat_axis=0, tiled=True)  29.1 us
    unnamed x70, local copies, waits for them, and re-layouts  24.5 us
    scatter-add x2, other arithmetic, feature_map(): columns[:, upper_j, :]  21.3 us
  transfers between devices with their start and end apart: 7, of which 6 were waited for; matrix products, arithmetic and copies ran while one was open for 3% of the time, Pallas kernels for 0%

profile of v1, /device:TPU:1, one launch (start us, length us, event | category | flops | bytes accessed | tf_op | source)
XLA Modules:
  0.0 773.1 jit_solution(16962347574090748644)
XLA Ops:
  8.1 4.0 collective-permute-start
  17.6 3.1 multiply_add_fusion.1
  20.7 6.1 all-to-all-start
  28.8 32.8 %all-to-all-done = f32[128,8,320]{0,2,1:T(8,128)S(1)} async-done(((f32[128,8,320]{0,2,1:T(8,128)}), f32[128,8,320]{0,2,1:T(8,128)S(1)}, u32[]{:S(2)}, u32[]{:S(2)}) %all-to-all-start) | async-done | bytes 1310752 | tf_op jit(solution)/shard_map/all_to_all | solution.py:236
  64.6 3.0 gather_fusion.1
  67.6 3.1 gather_fusion.2
  70.7 3.0 gather_fusion.3
  73.7 3.1 fusion.89
  76.8 4.2 fusion.98
  83.7 2.5 copy.231
  86.2 4.2 all-to-all-start.1
  90.5 29.1 %all-to-all-done.1 = f32[128,8,256]{0,2,1:T(8,128)} async-done(((f32[128,8,256]{0,2,1:T(8,128)}), f32[128,8,256]{0,2,1:T(8,128)}, u32[]{:S(2)}, u32[]{:S(2)}) %all-to-all-start.1) | async-done | bytes 1048608 | tf_op jit(solution)/shard_map/all_to_all | solution.py:237
  119.7 2.8 copy.232
  122.5 2.4 reshape.233
  127.7 2.5 copy.272
  130.2 45.0 %all-gather.6.cloned.1.call-done = f32[64,309,128]{2,1,0:T(8,128)} async-done(((f32[1,309,128]{2,1,0:T(8,128)}), f32[64,309,128]{2,1,0:T(8,128)}) %all-gather.6.cloned.1.call-update) | async-done | bytes 10125328 | tf_op jit(solution)/shard_map/all_gather | solution.py:32
  175.2 5.7 copy.306
  184.8 110.5 %while.46 = (s32[]{:T(128)}, f32[2,153,128]{2,1,0:T(8,128)S(1)}, f32[2,153]{1,0:T(2,128)S(1)}, f32[8,128,2,128]{1,0,3,2:T(8,128)}, f32[8,2,128]{2,1,0:T(2,128)S(...) while((s32[]{:T(128)}, f32[2,153,128]{2,1,0:T(8,128)S(1)}, ...), condition=%wide.region_10.11_spmd.clone, body=%wide.region_7.10_spmd.clone.sunk | while | flops 231664960 | bytes 3280461 | solution.py:150
  189.1 4.8 dynamic_update_slice.74
  202.9 4.8 dynamic_update_slice.74
  216.7 4.8 dynamic_update_slice.74
  230.5 4.8 dynamic_update_slice.74
  244.3 4.8 dynamic_update_slice.74
  258.1 4.8 dynamic_update_slice.74
  271.9 4.8 dynamic_update_slice.74
  285.6 4.8 dynamic_update_slice.74
  295.4 2.4 reshape.237
  302.3 2.8 fusion.81
  306.6 87.9 %all-gather.8.cloned.1.call-done = f32[64,309,128]{2,1,0:T(8,128)} async-done(((f32[1,309,128]{2,1,0:T(8,128)}), f32[64,309,128]{2,1,0:T(8,128)}) %all-gather.8.cloned.1.call-update) | async-done | bytes 10125328 | tf_op jit(solution)/shard_map/all_gather | solution.py:32
  394.6 5.7 copy.305
  404.9 114.0 %while.47 = (s32[]{:T(128)}, f32[2,153,128]{2,1,0:T(8,128)S(1)}, f32[2,153]{1,0:T(2,128)S(1)}, f32[8,2,153,128]{3,2,1,0:T(8,128)}, f32[8,2,153,128]{3,2,1,0:T(8,...) while((s32[]{:T(128)}, f32[2,153,128]{2,1,0:T(8,128)S(1)}, ...), condition=%wide.region_14.15_spmd.clone, body=%wide.region_13.14_spmd.clone.sunk | while | flops 462717824 | bytes 4866477 | solution.py:210
  412.1 2.0 fusion.190
  440.5 2.0 fusion.190
  483.2 2.0 fusion.190
  497.4 2.0 fusion.190
  518.8 2.0 copy.242
  527.4 6.0 fusion.85
  533.4 14.0 %scatter_fusion = f32[2,16,1024]{2,0,1:T(2,128)S(1)} fusion(f32[2,16,1024]{2,0,1:T(2,128)S(1)} %split.16, s32[136]{0:T(256)S(1)} %copy-done.21, f32[136,2,1024]{2,1,0:T(2,128)} %get-tuple-element.822), kind=kCustom, calls=%fused_computation.4 | custom fusion | flops 278528 | bytes 3342880 | tf_op jit(solution)/shard_map/transpose(jvp())/scatter-add | solution.py:49
  547.4 7.6 scatter_fusion.1
  556.2 7.6 scatter_fusion.3
  563.8 7.3 scatter_fusion.2
  572.6 2.7 pad_maximum_fusion
  576.9 40.8 %all_to_all.51 = f32[8,128,320]{1,2,0:T(8,128)S(1)} all-to-all(f32[8,128,320]{1,2,0:T(8,128)S(1)} %copy.248), channel_id=1, replica_groups=mesh['seq'=64,'head'=8] {'head'}, dimensions={0} | all-to-all | bytes 2621440 | tf_op jit(solution)/shard_map/all_to_all | solution.py:241
  617.8 2.2 multiply_reduce_fusion.2
  623.0 2.6 collective-permute-done.1
  627.1 4.4 fusion.75
  633.0 120.5 %all-gather.10.cloned.1.call-done = f32[512,3,2560]{2,1,0:T(4,128)} async-done(((f32[1,3,2560]{2,1,0:T(4,128)}), f32[512,3,2560]{2,1,0:T(4,128)}) %all-gather.10.cloned.1.call-update) | async-done | bytes 15728656 | tf_op jit(solution)/shard_map/all_gather | solution.py:246
  753.5 12.6 %reduce_sum.97 = f32[3,2560]{1,0:T(4,128)} reduce(f32[512,3,2560]{2,1,0:T(4,128)} %all-gather.10.cloned.1.call-done, f32[]{:T(128)} %constant.143.clone.1), dimensions={0}, to_apply=%region_22.23 | reduce | flops 3924480 | bytes 15759364 | tf_op jit(solution)/shard_map/reduce_sum | solution.py:246
  (438 shorter events, 202.1 us)
Async XLA Ops:
  8.1 9.1 %collective-permute-start = (f32[2,2560]{1,0:T(2,128)S(1)}, f32[2,2560]{1,0:T(2,128)S(1)}, u32[]{:S(2)}, u32[]{:S(2)}) collective-permute-start(f32[2,2560]{1,0:T(2,128)S(1)} %slice.116), channel_id=1, source_target_pairs={{0,1},{1,2},{2,3},{3,4},{4,5},{5,6},{6,7},{7,8},{8,9},{9,10},{10,1... | collective-permute-start | bytes 61448 | tf_op jit(solution)/shard_map/ppermute | solution.py:42
  14.4 3.2 copy-start.23
  14.4 3.2 copy-start.25
  15.4 2.2 copy-start.14
  15.4 2.2 copy-start.16
  15.4 2.2 copy-start.18
  17.1 3.6 copy-start.3
  17.6 3.1 copy-start.5
  20.7 7.4 copy-start.22
  20.7 7.4 copy-start.21
  20.7 40.9 %all-to-all-start = ((f32[128,8,320]{0,2,1:T(8,128)}), f32[128,8,320]{0,2,1:T(8,128)S(1)}, u32[]{:S(2)}, u32[]{:S(2)}) async-start(f32[128,8,320]{0,2,1:T(8,128)} %bitcast.250), calls=%async_computation | async-start | bytes 2621440 | tf_op jit(solution)/shard_map/all_to_all | solution.py:236
  26.8 148.4 %all-gather.6.cloned.1.call-start = ((), (), s32[]{:S(2)}) async-start(), calls=%async_computation.3 | async-start | bytes 10383360 | tf_op jit(solution)/shard_map/all_gather | solution.py:32
  27.0 63.5 %copy-start.20 = (s32[1026]{0:T(1024)}, s32[1026]{0:T(1024)S(1)}, u32[]{:S(2)}) copy-start(s32[1026]{0:T(1024)S(1)} %select_reduce_fusion) | copy-start | bytes 12316
  64.6 9.1 %copy-start.7 = (f32[136,2,1024]{2,1,0:T(2,128)}, f32[136,2,1024]{2,1,0:T(2,128)S(1)}, u32[]{:S(2)}) copy-start(f32[136,2,1024]{2,1,0:T(2,128)S(1)} %gather_fusion) | copy-start | bytes 3342340
  70.7 3.0 copy-start.27
  86.2 33.5 %all-to-all-start.1 = ((f32[128,8,256]{0,2,1:T(8,128)}), f32[128,8,256]{0,2,1:T(8,128)}, u32[]{:S(2)}, u32[]{:S(2)}) async-start(f32[128,8,256]{0,2,1:T(8,128)} %bitcast.257), calls=%async_computation.1 | async-start | bytes 2097152 | tf_op jit(solution)/shard_map/all_to_all | solution.py:237
  90.5 304.1 %all-gather.8.cloned.1.call-start = ((), (), s32[]{:S(2)}) async-start(), calls=%async_computation.4 | async-start | bytes 10383360 | tf_op jit(solution)/shard_map/all_gather | solution.py:32
  125.9 1.3 copy-start.10
  183.5 1.3 slice-start.1
  297.7 2.9 copy-start.2
  299.6 1.0 copy-start
  305.9 447.6 %all-gather.10.cloned.1.call-start = ((), (), s32[]{:S(2)}) async-start(), calls=%async_computation.5 | async-start | bytes 21012480 | tf_op jit(solution)/shard_map/all_gather | solution.py:246
  520.9 1.7 copy-start.9
  524.3 3.1 copy-start.8
  526.3 7.0 copy-start.1
  533.4 14.0 %copy-start.13 = (f32[136,2,1024]{2,1,0:T(2,128)S(1)}, f32[136,2,1024]{2,1,0:T(2,128)}, u32[]{:S(2)}) copy-start(f32[136,2,1024]{2,1,0:T(2,128)} %get-tuple-element.821) | copy-start | bytes 3342340
  555.0 1.2 copy-start.12
  556.2 7.6 slice-start
  556.2 7.6 copy-start.11
  576.6 41.1 %copy-start.24 = (f32[128]{0:T(128)S(1)}, f32[128]{0:T(128)}, u32[]{:S(2)}) copy-start(f32[128]{0:T(128)} %copy-done.23) | copy-start | bytes 1540
  576.6 41.1 %copy-start.26 = (f32[128]{0:T(128)S(1)}, f32[128]{0:T(128)}, u32[]{:S(2)}) copy-start(f32[128]{0:T(128)} %copy-done.25) | copy-start | bytes 1540
  576.9 40.8 %copy-start.4 = (f32[128,2560]{0,1:T(8,128)S(1)}, f32[128,2560]{0,1:T(8,128)}, u32[]{:S(2)}) copy-start(f32[128,2560]{0,1:T(8,128)} %copy-done.3) | copy-start | bytes 3932164
  576.9 40.8 %copy-start.6 = (f32[2,2560]{0,1:T(8,128)S(1)}, f32[2,2560]{0,1:T(8,128)}, u32[]{:S(2)}) copy-start(f32[2,2560]{0,1:T(8,128)} %copy-done.5) | copy-start | bytes 61444
  620.6 6.5 copy-start.15
  620.7 6.5 copy-start.17
  620.7 6.5 copy-start.19
  620.7 6.5 copy-start.28
  620.7 6.5 copy-start.29
  621.1 4.5 collective-permute-start.1
Sparse Core Ops, SparseCore 0:
  83.8 91.4 all-gather.5
  306.0 88.5 all-gather.7
  620.8 132.6 all-gather.9
